TPU v7x, 32 devices: a whole 2x2x4 slice. The times are simulated.
32 devices in a mesh: tx: 4 (over y, x), ty: 8 (over z, core).
Axes of the slice: x: 2, y: 2, z: 4, core: 2. Of those that a mesh axis runs over, the one named last changes fastest.
Arguments:
- stack: bfloat16 [32, 2, 128, 4096], P('tx', None, None, 'ty'), may hold values from -6 to 6
- filt_re: bfloat16 [32, 32], replicated, may hold values from -0.75 to 0.75
- filt_im: bfloat16 [32, 32], replicated, may hold values from -0.75 to 0.75
- pre_ids: int32 [32], replicated, may hold values from 0 to 15
- post_ids: int32 [32], replicated, may hold values from 16 to 31
Outputs:
- coherence: float32 [32, 128, 4096], P(None, 'ty', 'tx')
- change: float32 [32, 128, 4096], P(None, 'ty', 'tx')
All inputs are finite; a program needn't handle non-finite values.
Results may differ from a plain program's by a relative error of at most 0.0065.
Values may be sent and summed in bfloat16 or wider, within the bound.
No kernel may reach another device: no remote copies, remote signals or barrier semaphores. Data moves between devices by JAX's collectives and lax.ppermute only.
A program may use at most 128 MiB of HBM per device.

v0:
```python
import jax
import jax.numpy as jnp
from jax import lax
from jax.sharding import PartitionSpec as P

RADIUS = 4


def with_halo(block, sides, width):
    for axis, dim in sides:
        count = lax.axis_size(axis)
        forward = [(i, i + 1) for i in range(count - 1)]
        backward = [(target, source) for source, target in forward]
        low = lax.ppermute(
            lax.slice_in_dim(block, block.shape[dim] - width, None, axis=dim), axis, forward
        )
        high = lax.ppermute(lax.slice_in_dim(block, 0, width, axis=dim), axis, backward)
        block = jnp.concatenate([low, block, high], axis=dim)
    return block


def box_mean(fields, tile_rows, tile_cols, radius):
    window = 2 * radius + 1
    out_rows = jnp.arange(tile_rows)[:, None]
    in_rows = jnp.arange(tile_rows + 2 * radius)[None, :]
    row_gap = in_rows - out_rows
    row_band = jnp.where((row_gap >= 0) & (row_gap <= 2 * radius), 1.0, 0.0).astype(jnp.float32)
    in_cols = jnp.arange(tile_cols + 2 * radius)[:, None]
    out_cols = jnp.arange(tile_cols)[None, :]
    col_gap = in_cols - out_cols
    col_band = jnp.where((col_gap >= 0) & (col_gap <= 2 * radius), 1.0, 0.0).astype(jnp.float32)
    rowsum = jnp.einsum("ij,fjw->fiw", row_band, fields, precision=lax.Precision.HIGHEST)
    colsum = jnp.einsum("fiw,wk->fik", rowsum, col_band, precision=lax.Precision.HIGHEST)
    return colsum / float(window * window)


def pair_maps(padded, pre_ids, post_ids, tile_rows, tile_cols, radius):
    widened = padded.astype(jnp.float32)
    power = widened[:, 0] * widened[:, 0] + widened[:, 1] * widened[:, 1]
    pre_side = jnp.take(widened, pre_ids, axis=0)
    post_side = jnp.take(widened, post_ids, axis=0)
    cross_re = pre_side[:, 0] * post_side[:, 0] + pre_side[:, 1] * post_side[:, 1]
    cross_im = pre_side[:, 1] * post_side[:, 0] - pre_side[:, 0] * post_side[:, 1]
    fields = jnp.concatenate([power, cross_re, cross_im], axis=0)
    means = box_mean(fields, tile_rows, tile_cols, radius)
    count_acq = power.shape[0]
    count_pairs = pre_ids.shape[0]
    power_mean = means[:count_acq] + 1e-06
    pre_power = jnp.take(power_mean, pre_ids, axis=0)
    post_power = jnp.take(power_mean, post_ids, axis=0)
    real_mean = means[count_acq : count_acq + count_pairs]
    imag_mean = means[count_acq + count_pairs :]
    coherence = jnp.sqrt(real_mean * real_mean + imag_mean * imag_mean) / jnp.sqrt(
        pre_power * post_power
    )
    change = jnp.log(post_power / pre_power)
    return (coherence, change)


def shards(stack, filt_re, filt_im, pre_ids, post_ids):
    count_acq = filt_re.shape[0]
    mixing = jnp.stack([jnp.stack([filt_re, -filt_im], -1), jnp.stack([filt_im, filt_re], -1)], 1)
    mixing = mixing.reshape(2 * count_acq, 2 * count_acq)
    n_rows = lax.axis_size("ty")
    n_cols = lax.axis_size("tx")
    tile_rows = stack.shape[2] // n_rows
    tile_cols = stack.shape[3] * n_rows // n_cols
    by_rows = lax.all_to_all(stack, "ty", split_axis=2, concat_axis=3, tiled=True)
    piece = lax.all_to_all(by_rows, "tx", split_axis=3, concat_axis=0, tiled=True)
    height = piece.shape[2]
    breadth = piece.shape[3]
    flat = piece.reshape(2 * count_acq, height * breadth)
    result = jnp.dot(mixing, flat, preferred_element_type=jnp.float32)
    filtered = result.astype(jnp.bfloat16).reshape(count_acq, 2, height, breadth)
    padded = with_halo(filtered, (("tx", 3), ("ty", 2)), RADIUS)
    return pair_maps(padded, pre_ids, post_ids, tile_rows, tile_cols, RADIUS)


def solution(mesh):
    in_specs = (P("tx", None, None, "ty"), P(), P(), P(), P())
    out_specs = (P(None, "ty", "tx"), P(None, "ty", "tx"))
    return jax.shard_map(shards, mesh=mesh, in_specs=in_specs, out_specs=out_specs, check_vma=False)
```

profile of v0, /device:TPU:21, one launch (start us, length us, event | category | flops | bytes accessed | tf_op | source)
XLA Modules:
  0.0 292.3 jit_solution(7428069221730173030)
XLA Ops:
  0.6 2.8 copy.47
  3.4 50.5 %all_to_all.33 = bf16[8,2,128,512]{3,0,1,2:T(8,128)(2,1)S(1)} all-to-all(bf16[8,2,128,512]{3,0,1,2:T(8,128)(2,1)S(1)} %copy.47), channel_id=1, replica_groups=mesh['tx'=4,'ty'=8] {'ty'}, dimensions={2} | all-to-all | bytes 4194304 | tf_op jit(solution)/shard_map/all_to_all | solution.py:68
  53.9 20.2 %copy.58 = bf16[8,2,16,8,512]{2,1,0,4,3:T(2,128)(2,1)} copy(bf16[8,2,16,8,512]{4,0,1,2,3:T(8,128)(2,1)S(1)} %bitcast.50) | data formatting | bytes 4194304 | tf_op jit(solution)/shard_map/all_to_all | solution.py:68
  74.1 20.3 %reshape.82 = bf16[4,2,131072]{2,1,0:T(2,128)(2,1)} reshape(bf16[4096,8,2,16]{3,2,1,0:T(2,128)(2,1)} %bitcast.46) | data formatting | bytes 4194304
  94.4 3.9 %all-to-all-start.1 = ((bf16[4,2,131072]{2,1,0:T(2,128)(2,1)}), bf16[4,2,131072]{2,1,0:T(2,128)(2,1)S(1)}, u32[]{:S(2)}, u32[]{:S(2)}) async-start(bf16[4,2,131072]{2,1,0:T(2,128)(2,1)} %reshape.82), calls=%async_computation.1 | async-start | bytes 4194304 | tf_op jit(solution)/shard_map/all_to_all | solution.py:69
  99.8 22.2 %all-to-all-done.1 = bf16[4,2,131072]{2,1,0:T(2,128)(2,1)S(1)} async-done(((bf16[4,2,131072]{2,1,0:T(2,128)(2,1)}), bf16[4,2,131072]{2,1,0:T(2,128)(2,1)S(1)}, u32[]{:S(2)}, u32[]{:S(2)}) %all-to-all-start.1) | async-done | bytes 2097184 | tf_op jit(solution)/shard_map/all_to_all | solution.py:69
  122.0 13.4 %reshape.83 = bf16[4096,8,2,16]{3,2,1,0:T(2,128)(2,1)} reshape(bf16[4,2,131072]{2,1,0:T(2,128)(2,1)S(1)} %all-to-all-done.1) | data formatting | bytes 4194304
  135.4 35.3 %copy.50 = bf16[8,2,16,4,1024]{4,2,1,0,3:T(8,128)(2,1)S(1)} copy(bf16[8,2,16,4,1024]{2,1,0,4,3:T(2,128)(2,1)} %bitcast.47) | data formatting | bytes 4194304 | tf_op jit(solution)/shard_map/all_to_all | solution.py:69
  174.0 3.0 %collective-permute-start.1 = (bf16[32,2,16,4]{3,2,0,1:T(8,128)(2,1)S(1)}, bf16[32,2,16,4]{3,2,0,1:T(8,128)(2,1)S(1)}, u32[]{:S(2)}, u32[]{:S(2)}) collective-permute-start(bf16[32,2,16,4]{3,2,0,1:T(8,128)(2,1)S(1)} %get-tuple-element.10), channel_id=1, source_target_pairs={{8,0},{16,8},{24,16},{9,1},{17,9},{25,17},{10,2},{18,10},{26,18},{... | collective-permute-start | bytes 24584 | tf_op jit(solution)/shard_map/ppermute | solution.py:17
  177.0 2.3 collective-permute-start
  181.8 6.5 %collective-permute-done = bf16[32,2,16,4]{3,2,0,1:T(8,128)(2,1)S(1)} collective-permute-done((bf16[32,2,16,4]{3,2,0,1:T(8,128)(2,1)S(1)}, bf16[32,2,16,4]{3,2,0,1:T(8,128)(2,1)S(1)}, u32[]{:S(2)}, u32[]{:S(2)}) %collective-permute-start) | collective-permute-done | bytes 8224 | tf_op jit(solution)/shard_map/ppermute | solution.py:14
  188.3 4.8 %concatenate.9 = bf16[32,2,16,1032]{3,2,0,1:T(8,128)(2,1)S(1)} concatenate(bf16[32,2,16,4]{3,2,0,1:T(8,128)(2,1)S(1)} %collective-permute-done, bf16[32,2,16,1024]{3,2,0,1:T(8,128)(2,1)} %copy.51, bf16[32,2,16,4]{3,2,0,1:T(8,128)(2,1)S(1)} %collective-permute-done.1), dimensions={3} | concatenate | bytes 4227072 | tf_op jit(solution)/shard_map/concatenate | solution.py:18
  193.6 6.8 %collective-permute-start.2 = (bf16[32,2,4,1032]{3,2,0,1:T(4,128)(2,1)S(1)}, bf16[32,2,4,1032]{3,2,0,1:T(4,128)(2,1)S(1)}, u32[]{:S(2)}, u32[]{:S(2)}) collective-permute-start(bf16[32,2,4,1032]{3,2,0,1:T(4,128)(2,1)S(1)} %get-tuple-element.8), channel_id=1, source_target_pairs={{0,1},{1,2},{2,3},{3,4},{4,5},{5,6},{6,7},{8,9},{9,10},{10,11},{11... | collective-permute-start | bytes 1585160 | tf_op jit(solution)/shard_map/ppermute | solution.py:14
  202.5 4.6 %collective-permute-done.2 = bf16[32,2,4,1032]{3,2,0,1:T(4,128)(2,1)S(1)} collective-permute-done((bf16[32,2,4,1032]{3,2,0,1:T(4,128)(2,1)S(1)}, bf16[32,2,4,1032]{3,2,0,1:T(4,128)(2,1)S(1)}, u32[]{:S(2)}, u32[]{:S(2)}) %collective-permute-start.2) | collective-permute-done | bytes 528416 | tf_op jit(solution)/shard_map/ppermute | solution.py:14
  207.1 4.4 %collective-permute-done.3 = bf16[32,2,4,1032]{3,2,0,1:T(4,128)(2,1)S(1)} collective-permute-done((bf16[32,2,4,1032]{3,2,0,1:T(4,128)(2,1)S(1)}, bf16[32,2,4,1032]{3,2,0,1:T(4,128)(2,1)S(1)}, u32[]{:S(2)}, u32[]{:S(2)}) %collective-permute-start.3) | collective-permute-done | bytes 528416 | tf_op jit(solution)/shard_map/ppermute | solution.py:17
  215.3 3.4 %copy.54 = f32[32,2,24,1032]{3,2,1,0:T(8,128)} copy(f32[32,2,24,1032]{3,2,0,1:T(8,128)S(1)} %maximum_convert_fusion) | data formatting | bytes 12681216 | tf_op jit(solution)/shard_map/convert_element_type | solution.py:38
  218.7 7.0 %gather_fusion.1 = f32[32,2,24,1032]{3,2,1,0:T(8,128)} fusion(f32[32,2,24,1032]{3,2,1,0:T(8,128)} %copy.54, s32[1024]{0:T(1024)S(1)} %pad_clamp_fusion), kind=kCustom, calls=%fused_computation.2.clone | custom fusion | bytes 12681344 | tf_op jit(solution)/shard_map/jit(_take)/gather | solution.py:41
  225.7 6.8 %gather_fusion = f32[32,2,24,1032]{3,2,1,0:T(8,128)} fusion(f32[32,2,24,1032]{3,2,1,0:T(8,128)} %copy.54, s32[1024]{0:T(1024)S(1)} %pad_clamp_fusion.1), kind=kCustom, calls=%fused_computation.clone | custom fusion | bytes 12681344 | tf_op jit(solution)/shard_map/jit(_take)/gather | solution.py:40
  232.5 5.7 %copy_select_fusion = (f32[32,2,24,1032]{3,2,0,1:T(8,128)S(1)}, f32[32,2,24,1032]{3,2,0,1:T(8,128)S(1)}) fusion(f32[32,2,24,1032]{3,2,1,0:T(8,128)} %gather_fusion.1, pred[32]{0:T(512)(128)(4,1)S(1)} %compare_and_fusion, f32[32,2,24,1032]{3,2,1,0:T(8,128)} %gather_fusion, pred[32]{0:T(512)(128)(4,1)S(1)} %compare_and_fusion.1), kind=kLoop, calls=%fused_computation.13 | loop fusion | flops 3170304 | bytes 25362496 | tf_op jit(solution)/shard_map/jit(_take)/select_n | solution.py:41
  238.2 3.6 %add_bitcast_fusion = (f32[32,24,1032]{2,1,0:T(8,128)}, f32[32,24,1032]{2,1,0:T(8,128)}) fusion(f32[32,2,24,1032]{3,2,0,1:T(8,128)S(1)} %get-tuple-element.14, f32[32,2,24,1032]{3,2,0,1:T(8,128)S(1)} %get-tuple-element.15), kind=kLoop, calls=%fused_computation.27 | loop fusion | flops 4755456 | bytes 19021824 | tf_op jit(solution)/shard_map/add | solution.py:42
  241.8 9.5 %fusion = f32[96,1032,16]{1,2,0:T(8,128)S(1)} fusion(f32[32,24,1032]{2,1,0:T(8,128)} %get-tuple-element.5, f32[32,24,1032]{2,1,0:T(8,128)} %get-tuple-element.4, f32[32,24,1032]{2,1,0:T(8,128)} %fusion.16), kind=kOutput, calls=%fused_computation.5 | convolution fusion | flops 461281152 | bytes 15851520 | tf_op jit(solution)/shard_map/ij,fjw->fiw/dot_general | solution.py:32
  251.4 26.9 %broadcast_multiply_fusion = f32[96,16,1024]{2,1,0:T(8,128)S(1)} fusion(f32[96,1032,16]{1,2,0:T(8,128)S(1)} %fusion), kind=kOutput, calls=%fused_computation.28 | convolution fusion | flops 19485204480 | bytes 12632064 | tf_op jit(solution)/shard_map/fiw,wk->fik/dot_general | solution.py:33
  278.3 2.7 copy-done
  285.1 7.1 %divide_log_fusion = (f32[32,16,1024]{2,1,0:T(8,128)}, f32[32,16,1024]{2,1,0:T(8,128)}) fusion(f32[32,16,1024]{2,1,0:T(8,128)} %gather_fusion.3, f32[32,16,1024]{2,1,0:T(8,128)} %gather_fusion.2, pred[32]{0:T(512)(128)(4,1)S(1)} %compare_and_fusion, pred[32]{0:T(512)(128)(4,1)S(1)} %compare_and_fusion.1, f32[96,16,1024]{2,1,0:T(8,128)} %copy-done), kind=kLoop, calls=%fused_computation.39 | loop fusion | flops 4194304 | bytes 12582976 | tf_op jit(solution)/shard_map/log | solution.py:56
  (33 shorter events, 17.7 us)
Async XLA Ops:
  94.4 4.0 %copy-start.1 = (bf16[32,32]{1,0:T(8,128)(2,1)S(1)}, bf16[32,32]{1,0:T(8,128)(2,1)}, u32[]{:S(2)}) copy-start(bf16[32,32]{1,0:T(8,128)(2,1)} %param.11) | copy-start | bytes 6148
  94.4 4.0 %copy-start.2 = (bf16[32,32]{1,0:T(8,128)(2,1)S(1)}, bf16[32,32]{1,0:T(8,128)(2,1)}, u32[]{:S(2)}) copy-start(bf16[32,32]{1,0:T(8,128)(2,1)} %param.10) | copy-start | bytes 6148
  94.4 5.3 %copy-start.3 = (s32[32]{0:T(128)S(1)}, s32[32]{0:T(128)}, u32[]{:S(2)}) copy-start(s32[32]{0:T(128)} %param.12) | copy-start | bytes 388
  94.4 5.3 %copy-start.4 = (s32[32]{0:T(128)S(1)}, s32[32]{0:T(128)}, u32[]{:S(2)}) copy-start(s32[32]{0:T(128)} %param.13) | copy-start | bytes 388
  94.4 27.6 %all-to-all-start.1 = ((bf16[4,2,131072]{2,1,0:T(2,128)(2,1)}), bf16[4,2,131072]{2,1,0:T(2,128)(2,1)S(1)}, u32[]{:S(2)}, u32[]{:S(2)}) async-start(bf16[4,2,131072]{2,1,0:T(2,128)(2,1)} %reshape.82), calls=%async_computation.1 | async-start | bytes 4194304 | tf_op jit(solution)/shard_map/all_to_all | solution.py:69
  174.0 7.7 %collective-permute-start.1 = (bf16[32,2,16,4]{3,2,0,1:T(8,128)(2,1)S(1)}, bf16[32,2,16,4]{3,2,0,1:T(8,128)(2,1)S(1)}, u32[]{:S(2)}, u32[]{:S(2)}) collective-permute-start(bf16[32,2,16,4]{3,2,0,1:T(8,128)(2,1)S(1)} %get-tuple-element.10), channel_id=1, source_target_pairs={{8,0},{16,8},{24,16},{9,1},{17,9},{25,17},{10,2},{18,10},{26,18},{... | collective-permute-start | bytes 24584 | tf_op jit(solution)/shard_map/ppermute | solution.py:17
  177.0 11.2 %collective-permute-start = (bf16[32,2,16,4]{3,2,0,1:T(8,128)(2,1)S(1)}, bf16[32,2,16,4]{3,2,0,1:T(8,128)(2,1)S(1)}, u32[]{:S(2)}, u32[]{:S(2)}) collective-permute-start(bf16[32,2,16,4]{3,2,0,1:T(8,128)(2,1)S(1)} %get-tuple-element.11), channel_id=1, source_target_pairs={{0,8},{8,16},{16,24},{1,9},{9,17},{17,25},{2,10},{10,18},{18,26},{... | collective-permute-start | bytes 24584 | tf_op jit(solution)/shard_map/ppermute | solution.py:14
  193.6 13.6 %collective-permute-start.2 = (bf16[32,2,4,1032]{3,2,0,1:T(4,128)(2,1)S(1)}, bf16[32,2,4,1032]{3,2,0,1:T(4,128)(2,1)S(1)}, u32[]{:S(2)}, u32[]{:S(2)}) collective-permute-start(bf16[32,2,4,1032]{3,2,0,1:T(4,128)(2,1)S(1)} %get-tuple-element.8), channel_id=1, source_target_pairs={{0,1},{1,2},{2,3},{3,4},{4,5},{5,6},{6,7},{8,9},{9,10},{10,11},{11... | collective-permute-start | bytes 1585160 | tf_op jit(solution)/shard_map/ppermute | solution.py:14
  200.3 11.2 %collective-permute-start.3 = (bf16[32,2,4,1032]{3,2,0,1:T(4,128)(2,1)S(1)}, bf16[32,2,4,1032]{3,2,0,1:T(4,128)(2,1)S(1)}, u32[]{:S(2)}, u32[]{:S(2)}) collective-permute-start(bf16[32,2,4,1032]{3,2,0,1:T(4,128)(2,1)S(1)} %get-tuple-element.9), channel_id=1, source_target_pairs={{1,0},{2,1},{3,2},{4,3},{5,4},{6,5},{7,6},{9,8},{10,9},{11,10},{12... | collective-permute-start | bytes 1585160 | tf_op jit(solution)/shard_map/ppermute | solution.py:17
  278.3 2.7 copy-start
where the time goes:
time: 293 us; the launch traced here: 292 us
  local copies, waits for them, and re-layouts  127 us (43%)
  blocking collectives  50.5 us (17%)
  waiting for transfers between devices  38.6 us (13%)
  matrix products  37.1 us (13%)
  other arithmetic  20.5 us (7%)
  starting transfers between devices  18.1 us (6%)
    all_to_all x1, blocking collectives, shards(): lax.all_to_all(stack, 'ty', split_axis=2, concat_axis=3, tiled=True)  50.5 us
    unnamed x15, local copies, waits for them, and re-layouts  41.6 us
    all_to_all x1, local copies, waits for them, and re-layouts, shards(): lax.all_to_all(by_rows, 'tx', split_axis=3, concat_axis=0, tiled=True)  35.3 us
    dot_general x1, matrix products, box_mean(): jnp.einsum('fiw,wk->fik', rowsum, col_band, precision=lax.Precision.HIGHEST)  26.9 us
    all_to_all x1, waiting for transfers between devices, shards(): lax.all_to_all(by_rows, 'tx', split_axis=3, concat_axis=0, tiled=True)  22.2 us
    all_to_all x1, local copies, waits for them, and re-layouts, shards(): lax.all_to_all(stack, 'ty', split_axis=2, concat_axis=3, tiled=True)  20.2 us
    ppermute x2, waiting for transfers between devices, with_halo(): lax.ppermute(lax.slice_in_dim(block, block.shape[dim] - width, None, axis...  11.1 us
    dot_general x1, matrix products, box_mean(): jnp.einsum('ij,fjw->fiw', row_band, fields, precision=lax.Precision.HIGHEST)  9.53 us
  transfers between devices with their start and end apart: 5, of which 5 were waited for; matrix products, arithmetic and copies ran while one was open for 1% of the time, Pallas kernels for 0%

commit v1 on v0

--- a/solution.py
+++ b/solution.py
@@ -4,6 +4,13 @@
 from jax.sharding import PartitionSpec as P
 
 RADIUS = 4
+
+
+def trade_parts(value, name, split, join):
+    size = lax.axis_size(name)
+    blocks = jnp.stack(jnp.split(value, size, axis=split), axis=0)
+    blocks = lax.all_to_all(blocks, name, split_axis=0, concat_axis=0)
+    return jnp.concatenate(blocks, axis=join)
 
 
 def with_halo(block, sides, width):
@@ -66,7 +73,7 @@
     tile_rows = stack.shape[2] // n_rows
     tile_cols = stack.shape[3] * n_rows // n_cols
     by_rows = lax.all_to_all(stack, "ty", split_axis=2, concat_axis=3, tiled=True)
-    piece = lax.all_to_all(by_rows, "tx", split_axis=3, concat_axis=0, tiled=True)
+    piece = trade_parts(by_rows, "tx", 3, 0)
     height = piece.shape[2]
     breadth = piece.shape[3]
     flat = piece.reshape(2 * count_acq, height * breadth)

time: 293 us -> 211 us (0.72)
  local copies, waits for them, and re-layouts: 127 us -> 42.8 us
    all_to_all x1 -> x0, local copies, waits for them, and re-layouts: 35.3 us -> none  [shards(): lax.all_to_all(by_rows, 'tx', split_axis=3, concat_axis=0, tiled=True)]
    unnamed x15 -> x13, local copies, waits for them, and re-layouts: 41.6 us -> 7.85 us
    all_to_all x1 -> x2, local copies, waits for them, and re-layouts: 20.2 us -> 5.36 us  [shards(): lax.all_to_all(stack, 'ty', split_axis=2, concat_axis=3, tiled=True)]
where the time goes in v1:
time: 211 us; the launch traced here: 210 us
  blocking collectives  50.5 us (24%)
  local copies, waits for them, and re-layouts  42.8 us (20%)
  waiting for transfers between devices  38.7 us (18%)
  matrix products  37.1 us (18%)
  other arithmetic  22.1 us (10%)
  starting transfers between devices  18.1 us (9%)
    all_to_all x1, blocking collectives, shards(): lax.all_to_all(stack, 'ty', split_axis=2, concat_axis=3, tiled=True)  50.5 us
    dot_general x1, matrix products, box_mean(): jnp.einsum('fiw,wk->fik', rowsum, col_band, precision=lax.Precision.HIGHEST)  26.8 us
    all_to_all x1, waiting for transfers between devices, trade_parts(): blocks = lax.all_to_all(blocks, name, split_axis=0, concat_axis=0)  22.2 us
    ppermute x2, waiting for transfers between devices, with_halo(): lax.ppermute(lax.slice_in_dim(block, block.shape[dim] - width, None, axis...  11.1 us
    dot_general x1, matrix products, box_mean(): jnp.einsum('ij,fjw->fiw', row_band, fields, precision=lax.Precision.HIGHEST)  9.53 us
    ppermute x2, starting transfers between devices, with_halo(): lax.ppermute(lax.slice_in_dim(block, block.shape[dim] - width, None, axis...  9.06 us
    unnamed x13, local copies, waits for them, and re-layouts  7.85 us
    log x1, other arithmetic, pair_maps(): change = jnp.log(post_power / pre_power)  7.12 us
  transfers between devices with their start and end apart: 5, of which 5 were waited for; matrix products, arithmetic and copies ran while one was open for 1% of the time, Pallas kernels for 0%

profile of v1, /device:TPU:21, one launch (start us, length us, event | category | flops | bytes accessed | tf_op | source)
XLA Modules:
  0.0 210.1 jit_solution(862703232935006013)
XLA Ops:
  0.6 2.8 %copy.43 = bf16[8,2,128,512]{3,0,1,2:T(8,128)(2,1)S(1)} copy(bf16[8,2,128,512]{3,2,1,0:T(8,128)(2,1)} %param.9) | data formatting | bytes 4194304 | tf_op args[0]
  3.4 50.5 %all_to_all.23 = bf16[8,2,128,512]{3,0,1,2:T(8,128)(2,1)S(1)} all-to-all(bf16[8,2,128,512]{3,0,1,2:T(8,128)(2,1)S(1)} %copy.43), channel_id=1, replica_groups=mesh['tx'=4,'ty'=8] {'ty'}, dimensions={2} | all-to-all | bytes 4194304 | tf_op jit(solution)/shard_map/all_to_all | solution.py:75
  53.9 2.5 %copy.59 = bf16[8,2,8,16,512]{4,2,3,1,0:T(8,128)(2,1)} copy(bf16[8,2,8,16,512]{4,0,1,3,2:T(8,128)(2,1)S(1)} %bitcast.56) | data formatting | bytes 4194304 | tf_op jit(solution)/shard_map/all_to_all | solution.py:75
  56.4 2.9 %all_to_all.19 = bf16[8,2,16,4096]{3,2,1,0:T(8,128)(2,1)S(1)} reshape(bf16[8,2,16,8,512]{4,3,2,1,0:T(8,128)(2,1)} %bitcast.57) | data formatting | bytes 4194304 | tf_op jit(solution)/shard_map/all_to_all | solution.py:75
  61.0 3.9 %all-to-all-start.1 = ((bf16[4,8,2,16,1024]{4,3,2,1,0:T(8,128)(2,1)}), bf16[4,8,2,16,1024]{4,3,2,1,0:T(8,128)(2,1)S(1)}, u32[]{:S(2)}, u32[]{:S(2)}) async-start(bf16[4,8,2,16,1024]{4,3,2,1,0:T(8,128)(2,1)} %pad_maximum_fusion), calls=%async_computation.1 | async-start | bytes 4194304 | tf_op jit(solution)/shard_map/all_to_all | solution.py:12
  66.4 22.2 %all-to-all-done.1 = bf16[4,8,2,16,1024]{4,3,2,1,0:T(8,128)(2,1)S(1)} async-done(((bf16[4,8,2,16,1024]{4,3,2,1,0:T(8,128)(2,1)}), bf16[4,8,2,16,1024]{4,3,2,1,0:T(8,128)(2,1)S(1)}, u32[]{:S(2)}, u32[]{:S(2)}) %all-to-all-start.1) | async-done | bytes 2097184 | tf_op jit(solution)/shard_map/all_to_all | solution.py:12
  91.9 3.0 %collective-permute-start.1 = (bf16[32,2,16,4]{3,2,0,1:T(8,128)(2,1)S(1)}, bf16[32,2,16,4]{3,2,0,1:T(8,128)(2,1)S(1)}, u32[]{:S(2)}, u32[]{:S(2)}) collective-permute-start(bf16[32,2,16,4]{3,2,0,1:T(8,128)(2,1)S(1)} %get-tuple-element.10), channel_id=1, source_target_pairs={{8,0},{16,8},{24,16},{9,1},{17,9},{25,17},{10,2},{18,10},{26,18},{... | collective-permute-start | bytes 24584 | tf_op jit(solution)/shard_map/ppermute | solution.py:24
  94.9 2.3 %collective-permute-start = (bf16[32,2,16,4]{3,2,0,1:T(8,128)(2,1)S(1)}, bf16[32,2,16,4]{3,2,0,1:T(8,128)(2,1)S(1)}, u32[]{:S(2)}, u32[]{:S(2)}) collective-permute-start(bf16[32,2,16,4]{3,2,0,1:T(8,128)(2,1)S(1)} %get-tuple-element.11), channel_id=1, source_target_pairs={{0,8},{8,16},{16,24},{1,9},{9,17},{17,25},{2,10},{10,18},{18,26},{... | collective-permute-start | bytes 24584 | tf_op jit(solution)/shard_map/ppermute | solution.py:21
  99.6 6.5 %collective-permute-done = bf16[32,2,16,4]{3,2,0,1:T(8,128)(2,1)S(1)} collective-permute-done((bf16[32,2,16,4]{3,2,0,1:T(8,128)(2,1)S(1)}, bf16[32,2,16,4]{3,2,0,1:T(8,128)(2,1)S(1)}, u32[]{:S(2)}, u32[]{:S(2)}) %collective-permute-start) | collective-permute-done | bytes 8224 | tf_op jit(solution)/shard_map/ppermute | solution.py:21
  106.1 4.8 %concatenate.9 = bf16[32,2,16,1032]{3,2,0,1:T(8,128)(2,1)S(1)} concatenate(bf16[32,2,16,4]{3,2,0,1:T(8,128)(2,1)S(1)} %collective-permute-done, bf16[32,2,16,1024]{3,2,0,1:T(8,128)(2,1)} %copy.45, bf16[32,2,16,4]{3,2,0,1:T(8,128)(2,1)S(1)} %collective-permute-done.1), dimensions={3} | concatenate | bytes 4227072 | tf_op jit(solution)/shard_map/concatenate | solution.py:25
  111.4 6.8 %collective-permute-start.2 = (bf16[32,2,4,1032]{3,2,0,1:T(4,128)(2,1)S(1)}, bf16[32,2,4,1032]{3,2,0,1:T(4,128)(2,1)S(1)}, u32[]{:S(2)}, u32[]{:S(2)}) collective-permute-start(bf16[32,2,4,1032]{3,2,0,1:T(4,128)(2,1)S(1)} %get-tuple-element.8), channel_id=1, source_target_pairs={{0,1},{1,2},{2,3},{3,4},{4,5},{5,6},{6,7},{8,9},{9,10},{10,11},{11... | collective-permute-start | bytes 1585160 | tf_op jit(solution)/shard_map/ppermute | solution.py:21
  118.2 2.1 %collective-permute-start.3 = (bf16[32,2,4,1032]{3,2,0,1:T(4,128)(2,1)S(1)}, bf16[32,2,4,1032]{3,2,0,1:T(4,128)(2,1)S(1)}, u32[]{:S(2)}, u32[]{:S(2)}) collective-permute-start(bf16[32,2,4,1032]{3,2,0,1:T(4,128)(2,1)S(1)} %get-tuple-element.9), channel_id=1, source_target_pairs={{1,0},{2,1},{3,2},{4,3},{5,4},{6,5},{7,6},{9,8},{10,9},{11,10},{12... | collective-permute-start | bytes 1585160 | tf_op jit(solution)/shard_map/ppermute | solution.py:24
  120.3 4.7 %collective-permute-done.2 = bf16[32,2,4,1032]{3,2,0,1:T(4,128)(2,1)S(1)} collective-permute-done((bf16[32,2,4,1032]{3,2,0,1:T(4,128)(2,1)S(1)}, bf16[32,2,4,1032]{3,2,0,1:T(4,128)(2,1)S(1)}, u32[]{:S(2)}, u32[]{:S(2)}) %collective-permute-start.2) | collective-permute-done | bytes 528416 | tf_op jit(solution)/shard_map/ppermute | solution.py:21
  125.0 4.4 %collective-permute-done.3 = bf16[32,2,4,1032]{3,2,0,1:T(4,128)(2,1)S(1)} collective-permute-done((bf16[32,2,4,1032]{3,2,0,1:T(4,128)(2,1)S(1)}, bf16[32,2,4,1032]{3,2,0,1:T(4,128)(2,1)S(1)}, u32[]{:S(2)}, u32[]{:S(2)}) %collective-permute-start.3) | collective-permute-done | bytes 528416 | tf_op jit(solution)/shard_map/ppermute | solution.py:24
  131.1 2.1 %fusion.16 = f32[32,24,1032]{2,1,0:T(8,128)} fusion(f32[32,2,24,1032]{3,2,0,1:T(8,128)S(1)} %maximum_convert_fusion), kind=kLoop, calls=%fused_computation.23 | loop fusion | flops 2377728 | bytes 9510912 | tf_op jit(solution)/shard_map/add | solution.py:46
  133.2 3.4 %copy.48 = f32[32,2,24,1032]{3,2,1,0:T(8,128)} copy(f32[32,2,24,1032]{3,2,0,1:T(8,128)S(1)} %maximum_convert_fusion) | data formatting | bytes 12681216 | tf_op jit(solution)/shard_map/convert_element_type | solution.py:45
  136.6 6.9 %gather_fusion.1 = f32[32,2,24,1032]{3,2,1,0:T(8,128)} fusion(f32[32,2,24,1032]{3,2,1,0:T(8,128)} %copy.48, s32[1024]{0:T(1024)S(1)} %pad_clamp_fusion), kind=kCustom, calls=%fused_computation.2.clone | custom fusion | bytes 12681344 | tf_op jit(solution)/shard_map/jit(_take)/gather | solution.py:48
  143.5 6.8 %gather_fusion = f32[32,2,24,1032]{3,2,1,0:T(8,128)} fusion(f32[32,2,24,1032]{3,2,1,0:T(8,128)} %copy.48, s32[1024]{0:T(1024)S(1)} %pad_clamp_fusion.1), kind=kCustom, calls=%fused_computation.clone | custom fusion | bytes 12681344 | tf_op jit(solution)/shard_map/jit(_take)/gather | solution.py:47
  150.3 5.7 %copy_select_fusion = (f32[32,2,24,1032]{3,2,0,1:T(8,128)S(1)}, f32[32,2,24,1032]{3,2,0,1:T(8,128)S(1)}) fusion(f32[32,2,24,1032]{3,2,1,0:T(8,128)} %gather_fusion.1, pred[32]{0:T(512)(128)(4,1)S(1)} %compare_and_fusion, f32[32,2,24,1032]{3,2,1,0:T(8,128)} %gather_fusion, pred[32]{0:T(512)(128)(4,1)S(1)} %compare_and_fusion.1), kind=kLoop, calls=%fused_computation.13 | loop fusion | flops 3170304 | bytes 25362496 | tf_op jit(solution)/shard_map/jit(_take)/select_n | solution.py:48
  156.1 3.6 %add_bitcast_fusion = (f32[32,24,1032]{2,1,0:T(8,128)}, f32[32,24,1032]{2,1,0:T(8,128)}) fusion(f32[32,2,24,1032]{3,2,0,1:T(8,128)S(1)} %get-tuple-element.18, f32[32,2,24,1032]{3,2,0,1:T(8,128)S(1)} %get-tuple-element.19), kind=kLoop, calls=%fused_computation.27 | loop fusion | flops 4755456 | bytes 19021824 | tf_op jit(solution)/shard_map/add | solution.py:49
  159.7 9.5 %fusion = f32[96,1032,16]{1,2,0:T(8,128)S(1)} fusion(f32[32,24,1032]{2,1,0:T(8,128)} %get-tuple-element.5, f32[32,24,1032]{2,1,0:T(8,128)} %get-tuple-element.4, f32[32,24,1032]{2,1,0:T(8,128)} %fusion.16), kind=kOutput, calls=%fused_computation.5 | convolution fusion | flops 461281152 | bytes 15851520 | tf_op jit(solution)/shard_map/ij,fjw->fiw/dot_general | solution.py:39
  169.2 26.8 %broadcast_multiply_fusion = f32[96,16,1024]{2,1,0:T(8,128)S(1)} fusion(f32[96,1032,16]{1,2,0:T(8,128)S(1)} %fusion), kind=kOutput, calls=%fused_computation.28 | convolution fusion | flops 19485204480 | bytes 12632064 | tf_op jit(solution)/shard_map/fiw,wk->fik/dot_general | solution.py:40
  196.1 2.7 %copy-done = f32[96,16,1024]{2,1,0:T(8,128)} copy-done((f32[96,16,1024]{2,1,0:T(8,128)}, f32[96,16,1024]{2,1,0:T(8,128)S(1)}, u32[]{:S(2)}) %copy-start) | copy-done | bytes 6291480
  202.9 7.1 %divide_log_fusion = (f32[32,16,1024]{2,1,0:T(8,128)}, f32[32,16,1024]{2,1,0:T(8,128)}) fusion(f32[32,16,1024]{2,1,0:T(8,128)} %gather_fusion.3, f32[32,16,1024]{2,1,0:T(8,128)} %gather_fusion.2, pred[32]{0:T(512)(128)(4,1)S(1)} %compare_and_fusion, pred[32]{0:T(512)(128)(4,1)S(1)} %compare_and_fusion.1, f32[96,16,1024]{2,1,0:T(8,128)} %copy-done), kind=kLoop, calls=%fused_computation.41 | loop fusion | flops 4194304 | bytes 12582976 | tf_op jit(solution)/shard_map/log | solution.py:63
  (33 shorter events, 15.2 us)
Async XLA Ops:
  59.4 5.5 %copy-start.1 = (bf16[32,32]{1,0:T(8,128)(2,1)S(1)}, bf16[32,32]{1,0:T(8,128)(2,1)}, u32[]{:S(2)}) copy-start(bf16[32,32]{1,0:T(8,128)(2,1)} %param.11) | copy-start | bytes 6148
  59.4 5.5 %copy-start.2 = (bf16[32,32]{1,0:T(8,128)(2,1)S(1)}, bf16[32,32]{1,0:T(8,128)(2,1)}, u32[]{:S(2)}) copy-start(bf16[32,32]{1,0:T(8,128)(2,1)} %param.10) | copy-start | bytes 6148
  61.0 5.3 %copy-start.3 = (s32[32]{0:T(128)S(1)}, s32[32]{0:T(128)}, u32[]{:S(2)}) copy-start(s32[32]{0:T(128)} %param.12) | copy-start | bytes 388
  61.0 5.3 %copy-start.4 = (s32[32]{0:T(128)S(1)}, s32[32]{0:T(128)}, u32[]{:S(2)}) copy-start(s32[32]{0:T(128)} %param.13) | copy-start | bytes 388
  61.0 27.5 %all-to-all-start.1 = ((bf16[4,8,2,16,1024]{4,3,2,1,0:T(8,128)(2,1)}), bf16[4,8,2,16,1024]{4,3,2,1,0:T(8,128)(2,1)S(1)}, u32[]{:S(2)}, u32[]{:S(2)}) async-start(bf16[4,8,2,16,1024]{4,3,2,1,0:T(8,128)(2,1)} %pad_maximum_fusion), calls=%async_computation.1 | async-start | bytes 4194304 | tf_op jit(solution)/shard_map/all_to_all | solution.py:12
  91.9 7.8 %collective-permute-start.1 = (bf16[32,2,16,4]{3,2,0,1:T(8,128)(2,1)S(1)}, bf16[32,2,16,4]{3,2,0,1:T(8,128)(2,1)S(1)}, u32[]{:S(2)}, u32[]{:S(2)}) collective-permute-start(bf16[32,2,16,4]{3,2,0,1:T(8,128)(2,1)S(1)} %get-tuple-element.10), channel_id=1, source_target_pairs={{8,0},{16,8},{24,16},{9,1},{17,9},{25,17},{10,2},{18,10},{26,18},{... | collective-permute-start | bytes 24584 | tf_op jit(solution)/shard_map/ppermute | solution.py:24
  94.9 11.2 %collective-permute-start = (bf16[32,2,16,4]{3,2,0,1:T(8,128)(2,1)S(1)}, bf16[32,2,16,4]{3,2,0,1:T(8,128)(2,1)S(1)}, u32[]{:S(2)}, u32[]{:S(2)}) collective-permute-start(bf16[32,2,16,4]{3,2,0,1:T(8,128)(2,1)S(1)} %get-tuple-element.11), channel_id=1, source_target_pairs={{0,8},{8,16},{16,24},{1,9},{9,17},{17,25},{2,10},{10,18},{18,26},{... | collective-permute-start | bytes 24584 | tf_op jit(solution)/shard_map/ppermute | solution.py:21
  111.4 13.6 %collective-permute-start.2 = (bf16[32,2,4,1032]{3,2,0,1:T(4,128)(2,1)S(1)}, bf16[32,2,4,1032]{3,2,0,1:T(4,128)(2,1)S(1)}, u32[]{:S(2)}, u32[]{:S(2)}) collective-permute-start(bf16[32,2,4,1032]{3,2,0,1:T(4,128)(2,1)S(1)} %get-tuple-element.8), channel_id=1, source_target_pairs={{0,1},{1,2},{2,3},{3,4},{4,5},{5,6},{6,7},{8,9},{9,10},{10,11},{11... | collective-permute-start | bytes 1585160 | tf_op jit(solution)/shard_map/ppermute | solution.py:21
  118.2 11.2 %collective-permute-start.3 = (bf16[32,2,4,1032]{3,2,0,1:T(4,128)(2,1)S(1)}, bf16[32,2,4,1032]{3,2,0,1:T(4,128)(2,1)S(1)}, u32[]{:S(2)}, u32[]{:S(2)}) collective-permute-start(bf16[32,2,4,1032]{3,2,0,1:T(4,128)(2,1)S(1)} %get-tuple-element.9), channel_id=1, source_target_pairs={{1,0},{2,1},{3,2},{4,3},{5,4},{6,5},{7,6},{9,8},{10,9},{11,10},{12... | collective-permute-start | bytes 1585160 | tf_op jit(solution)/shard_map/ppermute | solution.py:24
  196.1 2.7 %copy-start = (f32[96,16,1024]{2,1,0:T(8,128)}, f32[96,16,1024]{2,1,0:T(8,128)S(1)}, u32[]{:S(2)}) copy-start(f32[96,16,1024]{2,1,0:T(8,128)S(1)} %broadcast_multiply_fusion) | copy-start | bytes 18874372
